TPU v7x, 32 devices: a whole 2x2x4 slice. The times are simulated.
32 devices in a mesh: leaf: 8 (over z, y), panel: 4 (over x, core).
Axes of the slice: x: 2, y: 2, z: 4, core: 2. Of those that a mesh axis runs over, the one named last changes fastest.
Arguments:
- interface_block: float32 [8, 2048, 2048], P('leaf', 'panel'), may hold values from -0.125 to 0.125
- coupling: bfloat16 [8, 2048, 128], P('leaf', 'panel'), may hold values from -0.375 to 0.375
- eigenvalues: float32 [8, 128], P('leaf'), may hold values from 0.5 to 8
- mode_counts: int32 [8], P('leaf'), may hold values from 64 to 128, as said below
- interface_coords: bfloat16 [8, 2048, 1024], P('leaf', 'panel'), may hold values from -6 to 6
- modal_coords: bfloat16 [8, 128, 4096], P('leaf'), may hold values from -6 to 6
Outputs:
- mode_shapes: float32 [8, 2048, 1024], P('leaf', 'panel')
Inputs may be any that keep to these rules, and one draw needn't show every extreme that they name: `mode_counts`: modes kept by each substructure; some substructure keeps all 128.
All inputs are finite; a program needn't handle non-finite values.
Results may differ from a plain program's by a relative error of at most 0.0023.
Values may be sent and summed in bfloat16 or wider, within the bound.
No kernel may reach another device: no remote copies, remote signals or barrier semaphores. Data moves between devices by JAX's collectives and lax.ppermute only.
A program may use at most 128 MiB of HBM per device.

v0:
```python
import jax
import jax.numpy as jnp
from jax import lax
from jax.sharding import Mesh, PartitionSpec as P


def on_device(interface_block, coupling, eigenvalues, mode_counts, interface_coords, modal_coords):
    block = interface_block[0]
    coup = coupling[0]
    coords = interface_coords[0]
    modal = modal_coords[0]
    width = coup.shape[1]
    group = lax.axis_size("leafin")
    index = jnp.arange(width, dtype=jnp.int32)
    mask = (index < mode_counts[0]).astype(jnp.float32)
    scaled = (coup.astype(jnp.float32) * (mask / eigenvalues[0])[None, :]).astype(jnp.bfloat16)
    dense = lax.psum(block, "leafin")
    scaled_all = lax.all_gather(scaled, "leafin", axis=1, tiled=True)
    coup_rows = lax.all_gather(coup, "panel", axis=0, tiled=True)
    coup_all = lax.all_gather(coup_rows, "leafin", axis=1, tiled=True)
    low = lax.dot_general(
        scaled_all, coup_all, (((1,), (1,)), ((), ())), preferred_element_type=jnp.float32
    )
    merged = dense - low
    rl = modal.shape[1] // group
    parts = jnp.transpose(modal.reshape(modal.shape[0], group, rl), (1, 0, 2))
    recv = lax.all_to_all(parts, "leafin", 0, 0, tiled=True)
    modal_term = jnp.dot(
        scaled_all, recv.reshape(group * modal.shape[0], rl), preferred_element_type=jnp.float32
    )
    coords_all = lax.all_gather(coords, "panel", axis=0, tiled=True)
    shapes = modal_term + jnp.dot(
        merged, coords_all.astype(jnp.float32), precision=lax.Precision.HIGHEST
    )
    return shapes[None]


def solution(mesh):

    def run(*args):
        group = args[5].shape[2] // args[4].shape[2]
        leaves, panels = (mesh.shape["leaf"], mesh.shape["panel"])
        grid = mesh.devices.reshape(leaves // group, group, panels)
        sub = Mesh(grid, ("grp", "leafin", "panel"))
        leaf = ("grp", "leafin")
        placed = (
            P(leaf, "panel", None),
            P(leaf, "panel", None),
            P(leaf, None),
            P(leaf),
            P(leaf, "panel", None),
            P(leaf, None, None),
        )
        body = jax.shard_map(
            on_device, mesh=sub, in_specs=placed, out_specs=P(leaf, "panel", None), check_vma=False
        )
        return body(*args)

    return run
```

profile of v0, /device:TPU:0, one launch (start us, length us, event | category | flops | bytes accessed | tf_op | source)
XLA Modules:
  0.0 295.3 jit_solution(14571388144809049129)
XLA Ops:
  6.5 0.0 copy-start
  6.5 0.0 all-gather.6.cloned.1.call-start
  6.5 10.3 %all-gather = bf16[1,2048,128]{2,1,0:T(8,128)(2,1)} all-gather(bf16[1,512,128]{2,1,0:T(8,128)(2,1)} %param.7), channel_id=2, replica_groups=mesh['grp'=2,'leafin'=4,'panel'=4] {'panel'}, dimensions={1}, use_global_device_ids=true | all-gather | bytes 655360 | tf_op jit(solution)/shard_map/all_gather | solution.py:19
  16.9 0.0 all-gather.6.cloned.1.call-update
  16.9 0.0 all-reduce.2.cloned.1.call-start
  16.9 0.0 copy-start.2
  16.9 0.0 copy-start.1
  17.0 0.7 all-reduce.2.cloned.1.call-update
  17.6 0.0 all-gather.8.cloned.1.call-start
  17.7 0.7 all-gather.8.cloned.1.call-update
  18.4 0.0 copy-done
  18.4 1.3 copy.7
  19.7 3.8 %all-to-all-start = ((bf16[4,128,1024]{1,2,0:T(8,128)(2,1)}), bf16[4,128,1024]{1,2,0:T(8,128)(2,1)S(1)}, u32[]{:S(2)}, u32[]{:S(2)}) async-start(bf16[4,128,1024]{1,2,0:T(8,128)(2,1)} %bitcast.4), calls=%async_computation | async-start | bytes 2097152 | tf_op jit(solution)/shard_map/all_to_all | solution.py:27
  24.1 0.0 copy-done.2
  24.2 0.0 copy-done.1
  24.2 57.9 %all_gather.12 = bf16[512,512]{1,0:T(8,128)(2,1)S(1)} all-gather(bf16[512,128]{1,0:T(8,128)(2,1)S(1)} %fusion.5), channel_id=1, replica_groups=mesh['grp'=2,'leafin'=4,'panel'=4] {'leafin'}, dimensions={1}, use_global_device_ids=true | all-gather | bytes 655360 | tf_op jit(solution)/shard_map/all_gather | solution.py:18
  82.1 0.0 all-to-all-done
  82.1 0.5 copy.8
  82.6 0.0 all-gather.6.cloned.1.call-done
  82.7 4.8 %fusion.3 = f32[512,2048]{1,0:T(8,128)} fusion(bf16[512,512]{1,0:T(8,128)(2,1)S(1)} %all_gather.12, bf16[1,2048,512]{2,1,0:T(8,128)(2,1)} %all-gather.6.cloned.1.call-done), kind=kOutput, calls=%fused_computation.3 | convolution fusion | flops 1073741824 | bytes 6815744 | tf_op jit(solution)/shard_map/dot_general | solution.py:21
  87.5 152.8 %all-reduce.2.cloned.1.call-done = f32[512,2048]{1,0:T(8,128)} async-done(((f32[512,2048]{1,0:T(8,128)}), f32[512,2048]{1,0:T(8,128)}) %all-reduce.2.cloned.1.call-update) | async-done | bytes 4194320 | tf_op jit(solution)/shard_map/psum | solution.py:17
  240.3 35.9 %all-gather.8.cloned.1.call-done = bf16[1,2048,1024]{2,1,0:T(8,128)(2,1)} async-done(((bf16[1,512,1024]{2,1,0:T(8,128)(2,1)}), bf16[1,2048,1024]{2,1,0:T(8,128)(2,1)}) %all-gather.8.cloned.1.call-update) | async-done | bytes 4194320 | tf_op jit(solution)/shard_map/all_gather | solution.py:31
  276.3 10.5 %fusion = f32[512,1024]{1,0:T(8,128)S(1)} fusion(bf16[1,2048,1024]{2,1,0:T(8,128)(2,1)} %all-gather.8.cloned.1.call-done, f32[512,2048]{1,0:T(8,128)} %all-reduce.2.cloned.1.call-done, f32[512,2048]{1,0:T(8,128)} %fusion.3), kind=kOutput, calls=%fused_computation | convolution fusion | flops 12885950464 | bytes 14680064 | tf_op jit(solution)/shard_map/dot_general | solution.py:32
  286.7 2.0 add_bitcast_fusion
  (2 shorter events, 0.0 us)
Async XLA Ops:
  6.5 11.8 %copy-start = (bf16[1,128,4096]{2,1,0:T(8,128)(2,1)S(1)}, bf16[1,128,4096]{2,1,0:T(8,128)(2,1)}, u32[]{:S(2)}) copy-start(bf16[1,128,4096]{2,1,0:T(8,128)(2,1)} %param.11) | copy-start | bytes 3145732
  6.5 76.1 %all-gather.6.cloned.1.call-start = ((), (), s32[]{:S(2)}) async-start(), calls=%async_computation.2 | async-start | bytes 2621440 | tf_op jit(solution)/shard_map/all_gather | solution.py:20
  16.9 223.5 %all-reduce.2.cloned.1.call-start = ((), (), s32[]{:S(2)}) async-start(), calls=%async_computation.1 | async-start | bytes 8388608 | tf_op jit(solution)/shard_map/psum | solution.py:17
  16.9 7.2 %copy-start.2 = (f32[1,128]{1,0:T(1,128)S(1)}, f32[1,128]{1,0:T(1,128)}, u32[]{:S(2)}) copy-start(f32[1,128]{1,0:T(1,128)} %param.8) | copy-start | bytes 1540
  16.9 7.2 %copy-start.1 = (bf16[1,512,128]{2,1,0:T(8,128)(2,1)S(1)}, bf16[1,512,128]{2,1,0:T(8,128)(2,1)}, u32[]{:S(2)}) copy-start(bf16[1,512,128]{2,1,0:T(8,128)(2,1)} %param.7) | copy-start | bytes 393220
  17.6 258.6 %all-gather.8.cloned.1.call-start = ((), (), s32[]{:S(2)}) async-start(), calls=%async_computation.3 | async-start | bytes 5242880 | tf_op jit(solution)/shard_map/all_gather | solution.py:31
  19.7 62.4 %all-to-all-start = ((bf16[4,128,1024]{1,2,0:T(8,128)(2,1)}), bf16[4,128,1024]{1,2,0:T(8,128)(2,1)S(1)}, u32[]{:S(2)}, u32[]{:S(2)}) async-start(bf16[4,128,1024]{1,2,0:T(8,128)(2,1)} %bitcast.4), calls=%async_computation | async-start | bytes 2097152 | tf_op jit(solution)/shard_map/all_to_all | solution.py:27
Sparse Core Ops, SparseCore 0:
  17.0 65.2 all-gather.5
  84.7 155.6 all-reduce.1
  241.9 34.2 all-gather.7
where the time goes:
time: 296 us; the launch traced here: 295 us
  waiting for transfers between devices  190 us (64%)
  blocking collectives  68.2 us (23%)
  matrix products  17.3 us (6%)
  between operations  13.8 us (5%)
  starting transfers between devices  3.88 us (1%)
    psum x1, waiting for transfers between devices, on_device(): dense = lax.psum(block, 'leafin')  153 us
    all_gather x1, blocking collectives, on_device(): scaled_all = lax.all_gather(scaled, 'leafin', axis=1, tiled=True)  57.9 us
    all_gather x1, waiting for transfers between devices, on_device(): coords_all = lax.all_gather(coords, 'panel', axis=0, tiled=True)  35.9 us
    dot_general x1, matrix products, on_device(): jnp.dot(merged, coords_all.astype(jnp.float32), precision=lax.Precision.H...  10.5 us
    all_gather x1, blocking collectives, on_device(): coup_rows = lax.all_gather(coup, 'panel', axis=0, tiled=True)  10.3 us
  transfers between devices with their start and end apart: 4, of which 2 were waited for; matrix products, arithmetic and copies ran while one was open for 2% of the time, Pallas kernels for 0%

commit v1 on v0

--- a/solution.py
+++ b/solution.py
@@ -14,7 +14,7 @@
     index = jnp.arange(width, dtype=jnp.int32)
     mask = (index < mode_counts[0]).astype(jnp.float32)
     scaled = (coup.astype(jnp.float32) * (mask / eigenvalues[0])[None, :]).astype(jnp.bfloat16)
-    dense = lax.psum(block, "leafin")
+    dense = jnp.sum(lax.all_gather(block, "leafin"), axis=0)
     scaled_all = lax.all_gather(scaled, "leafin", axis=1, tiled=True)
     coup_rows = lax.all_gather(coup, "panel", axis=0, tiled=True)
     coup_all = lax.all_gather(coup_rows, "leafin", axis=1, tiled=True)

time: 296 us -> 425 us (1.44)
  waiting for transfers between devices: 190 us -> 309 us
  other arithmetic: 0.04 us -> 10.4 us
    all_gather x0 -> x1, waiting for transfers between devices: none -> 283 us  [on_device(): dense = jnp.sum(lax.all_gather(block, 'leafin'), axis=0)]
    psum x1 -> x0, waiting for transfers between devices: 153 us -> none  [on_device(): dense = lax.psum(block, 'leafin')]
    all_gather x1, waiting for transfers between devices: 35.9 us -> 24.8 us  [on_device(): coords_all = lax.all_gather(coords, 'panel', axis=0, tiled=True)]
    reduce_sum x0 -> x1, other arithmetic: none -> 10.3 us  [on_device(): dense = jnp.sum(lax.all_gather(block, 'leafin'), axis=0)]
  transfers between devices with their start and end apart: 4 -> 4, of which waited for: 2 -> 2; matrix products, arithmetic and copies ran while one was open for 2% -> 4% of each run, Pallas kernels for 0% -> 0%
where the time goes in v1:
time: 425 us
  waiting for transfers between devices  309 us (73%)
  blocking collectives  68.2 us (16%)
  matrix products  17.3 us (4%)
  between operations  13.8 us (3%)
  other arithmetic  10.4 us (2%)
    all_gather x1, waiting for transfers between devices, on_device(): dense = jnp.sum(lax.all_gather(block, 'leafin'), axis=0)  283 us
    all_gather x1, blocking collectives, on_device(): scaled_all = lax.all_gather(scaled, 'leafin', axis=1, tiled=True)  57.9 us
    all_gather x1, waiting for transfers between devices, on_device(): coords_all = lax.all_gather(coords, 'panel', axis=0, tiled=True)  24.8 us
    dot_general x1, matrix products, on_device(): jnp.dot(merged, coords_all.astype(jnp.float32), precision=lax.Precision.H...  10.5 us
    reduce_sum x1, other arithmetic, on_device(): dense = jnp.sum(lax.all_gather(block, 'leafin'), axis=0)  10.3 us
    all_gather x1, blocking collectives, on_device(): coup_rows = lax.all_gather(coup, 'panel', axis=0, tiled=True)  10.3 us
  transfers between devices with their start and end apart: 4, of which 2 were waited for; matrix products, arithmetic and copies ran while one was open for 4% of the time, Pallas kernels for 0%

profile of v1, /device:TPU:0, one launch (start us, length us, event | category | flops | bytes accessed | tf_op | source)
XLA Modules:
  0.0 424.8 jit_solution(6572633663323587576)
XLA Ops:
  6.5 0.0 copy-start
  6.5 0.0 all-gather.9.cloned.1.call-start
  6.5 10.3 %all-gather = bf16[1,2048,128]{2,1,0:T(8,128)(2,1)} all-gather(bf16[1,512,128]{2,1,0:T(8,128)(2,1)} %param.7), channel_id=2, replica_groups=mesh['grp'=2,'leafin'=4,'panel'=4] {'panel'}, dimensions={1}, use_global_device_ids=true | all-gather | bytes 655360 | tf_op jit(solution)/shard_map/all_gather | solution.py:19
  16.9 0.0 all-gather.9.cloned.1.call-update
  16.9 0.0 copy-start.2
  16.9 0.0 copy-start.1
  16.9 0.0 all-gather.7.cloned.1.call-start
  16.9 0.7 all-gather.7.cloned.1.call-update
  17.7 0.0 all-gather.11.cloned.1.call-start
  17.7 0.7 all-gather.11.cloned.1.call-update
  18.4 0.0 copy-done
  18.4 1.3 copy.9
  19.7 3.8 all-to-all-start
  24.2 0.0 copy-done.2
  24.2 0.0 copy-done.1
  24.2 57.9 %all_gather.15 = bf16[512,512]{1,0:T(8,128)(2,1)S(1)} all-gather(bf16[512,128]{1,0:T(8,128)(2,1)S(1)} %fusion.5), channel_id=1, replica_groups=mesh['grp'=2,'leafin'=4,'panel'=4] {'leafin'}, dimensions={1}, use_global_device_ids=true | all-gather | bytes 655360 | tf_op jit(solution)/shard_map/all_gather | solution.py:18
  82.1 0.0 all-to-all-done
  82.1 0.5 copy.10
  82.7 0.0 all-gather.9.cloned.1.call-done
  82.7 4.8 %fusion.3 = f32[512,2048]{1,0:T(8,128)} fusion(bf16[512,512]{1,0:T(8,128)(2,1)S(1)} %all_gather.15, bf16[1,2048,512]{2,1,0:T(8,128)(2,1)} %all-gather.9.cloned.1.call-done), kind=kOutput, calls=%fused_computation.3 | convolution fusion | flops 1073741824 | bytes 6815744 | tf_op jit(solution)/shard_map/dot_general | solution.py:21
  87.5 283.1 %all-gather.7.cloned.1.call-done = f32[4,512,2048]{2,1,0:T(8,128)} async-done(((f32[1,512,2048]{2,1,0:T(8,128)}), f32[4,512,2048]{2,1,0:T(8,128)}) %all-gather.7.cloned.1.call-update) | async-done | bytes 16777232 | tf_op jit(solution)/shard_map/all_gather | solution.py:17
  370.7 10.3 %reduce_sum.9 = f32[512,2048]{1,0:T(8,128)} reduce(f32[4,512,2048]{2,1,0:T(8,128)} %all-gather.7.cloned.1.call-done, f32[]{:T(128)} %constant.0.clone.1), dimensions={0}, to_apply=%region_0.0 | reduce | flops 3145728 | bytes 20971524 | tf_op jit(solution)/shard_map/reduce_sum | solution.py:17
  381.0 24.8 %all-gather.11.cloned.1.call-done = bf16[1,2048,1024]{2,1,0:T(8,128)(2,1)} async-done(((bf16[1,512,1024]{2,1,0:T(8,128)(2,1)}), bf16[1,2048,1024]{2,1,0:T(8,128)(2,1)}) %all-gather.11.cloned.1.call-update) | async-done | bytes 4194320 | tf_op jit(solution)/shard_map/all_gather | solution.py:31
  405.8 10.5 %fusion = f32[512,1024]{1,0:T(8,128)S(1)} fusion(bf16[1,2048,1024]{2,1,0:T(8,128)(2,1)} %all-gather.11.cloned.1.call-done, f32[512,2048]{1,0:T(8,128)} %reduce_sum.9, f32[512,2048]{1,0:T(8,128)} %fusion.3), kind=kOutput, calls=%fused_computation | convolution fusion | flops 12885950464 | bytes 14680064 | tf_op jit(solution)/shard_map/dot_general | solution.py:32
  416.3 2.0 add_bitcast_fusion
  (2 shorter events, 0.0 us)
Async XLA Ops:
  6.5 11.9 %copy-start = (bf16[1,128,4096]{2,1,0:T(8,128)(2,1)S(1)}, bf16[1,128,4096]{2,1,0:T(8,128)(2,1)}, u32[]{:S(2)}) copy-start(bf16[1,128,4096]{2,1,0:T(8,128)(2,1)} %param.11) | copy-start | bytes 3145732
  6.5 76.1 %all-gather.9.cloned.1.call-start = ((), (), s32[]{:S(2)}) async-start(), calls=%async_computation.2 | async-start | bytes 2621440 | tf_op jit(solution)/shard_map/all_gather | solution.py:20
  16.9 7.3 %copy-start.2 = (f32[1,128]{1,0:T(1,128)S(1)}, f32[1,128]{1,0:T(1,128)}, u32[]{:S(2)}) copy-start(f32[1,128]{1,0:T(1,128)} %param.8) | copy-start | bytes 1540
  16.9 7.3 %copy-start.1 = (bf16[1,512,128]{2,1,0:T(8,128)(2,1)S(1)}, bf16[1,512,128]{2,1,0:T(8,128)(2,1)}, u32[]{:S(2)}) copy-start(bf16[1,512,128]{2,1,0:T(8,128)(2,1)} %param.7) | copy-start | bytes 393220
  16.9 353.8 %all-gather.7.cloned.1.call-start = ((), (), s32[]{:S(2)}) async-start(), calls=%async_computation.1 | async-start | bytes 20971520 | tf_op jit(solution)/shard_map/all_gather | solution.py:17
  17.7 388.2 %all-gather.11.cloned.1.call-start = ((), (), s32[]{:S(2)}) async-start(), calls=%async_computation.3 | async-start | bytes 5242880 | tf_op jit(solution)/shard_map/all_gather | solution.py:31
  19.7 62.4 %all-to-all-start = ((bf16[4,128,1024]{1,2,0:T(8,128)(2,1)}), bf16[4,128,1024]{1,2,0:T(8,128)(2,1)S(1)}, u32[]{:S(2)}, u32[]{:S(2)}) async-start(bf16[4,128,1024]{1,2,0:T(8,128)(2,1)} %bitcast.4), calls=%async_computation | async-start | bytes 2097152 | tf_op jit(solution)/shard_map/all_to_all | solution.py:27
Sparse Core Ops, SparseCore 0:
  17.0 65.2 all-gather.8
  83.8 286.8 all-gather.6
  372.2 33.5 all-gather.10
